TPU v7x, 32 devices: a whole 2x2x4 slice. The times are simulated.
32 devices in a mesh: groups: 2 (over y), area: 4 (over z), neuron: 4 (over x, core).
Axes of the slice: x: 2, y: 2, z: 4, core: 2. Of those that a mesh axis runs over, the one named last changes fastest.
Arguments:
- window: bfloat16 [32, 16, 32768], P(None, 'groups', ('area', 'neuron')), parts along dimension 1, may hold values from -6 to 6
- err_grad: float32 [16, 16, 32768], P(None, 'groups', ('area', 'neuron')), parts along dimension 1, may hold values from -6 to 6
- surrogate: float32 [16, 16, 32768], P(None, 'groups', ('area', 'neuron')), parts along dimension 1, may hold values from 0 to 0.5
- lv_end: float32 [16, 32768], P('groups', ('area', 'neuron')), parts along dimension 0, may hold values from -6 to 6
- la_end: float32 [16, 32768], P('groups', ('area', 'neuron')), parts along dimension 0, may hold values from -6 to 6
- alpha: float32 [32768], P(('area', 'neuron')), may hold values from 0.8 to 0.99
- rho: float32 [32768], P(('area', 'neuron')), may hold values from 0.9 to 0.999
- beta: float32 [32768], P(('area', 'neuron')), may hold values from 0.3 to 2
- weights: bfloat16 [4, 4, 64, 4, 128, 128], P(None, 'area', 'neuron'), may hold values from -0.25 to 0.25
- block_index: int32 [4, 4, 64, 4], P(None, 'area', 'neuron'), may hold values from 0 to 63, as said below
- delays: int32 [4, 4], replicated, may hold values from 16 to 31, as said below
Outputs:
- cur_adjoint: bfloat16 [16, 16, 32768], P(None, 'groups', ('area', 'neuron')), parts along dimension 1
- lv_start: float32 [16, 32768], P('groups', ('area', 'neuron')), parts along dimension 0
- la_start: float32 [16, 32768], P('groups', ('area', 'neuron')), parts along dimension 0
There are 2 independent parts, one for each index of `groups`. A program takes and returns all parts, laid end to end along the dimension named above; an argument that names none is the same for every part. Nothing has to cross between parts.
Inputs may be any that keep to these rules, and one draw needn't show every extreme that they name: `delays`: every entry lies in 16 to 31 and both ends occur. `block_index`: both ends occur.
All inputs are finite; a program needn't handle non-finite values.
Results may differ from a plain program's by a relative error of at most 0.001.
Values may be sent and summed in bfloat16 or wider, within the bound.
No kernel may reach another device: no remote copies, remote signals or barrier semaphores. Data moves between devices by JAX's collectives and lax.ppermute only.
A program may use at most 64 MiB of HBM per device.

v0:
```python
import jax
import jax.numpy as jnp
from jax import lax
from jax.sharding import PartitionSpec as P


def partner(value, axis, bit):
    mask = 2**bit
    pairs = [(source, source ^ mask) for source in range(lax.axis_size(axis))]
    return lax.ppermute(value, axis, pairs)


def adjoint_scan(err_grad, surrogate, rec, lv_end, la_end, alpha, rho, beta):

    def step(carry, inputs):
        lv_now, la_now = carry
        error_t, surr_t, rec_t = inputs
        total = error_t + rec_t - lv_now + la_now
        lv_next = alpha * lv_now + surr_t * total
        la_next = rho * la_now - beta * surr_t * total
        return ((lv_next, la_next), lv_now.astype(jnp.bfloat16))

    (lv_start, la_start), currents = lax.scan(
        step, (lv_end, la_end), (err_grad, surrogate, rec), reverse=True
    )
    return (currents, lv_start, la_start)


def per_device(
    window, err_grad, surrogate, lv_end, la_end, alpha, rho, beta, weights, block_index, delays
):
    steps = err_grad.shape[0]
    batch = err_grad.shape[1]
    local_neurons = err_grad.shape[2]
    block_side = weights.shape[-1]
    rounds = weights.shape[0]
    levels = lax.axis_size("area").bit_length() - 1
    me_area = lax.axis_index("area")
    rec = jnp.zeros((steps * batch, local_neurons), jnp.float32)
    for rnd in range(rounds):
        bit = rnd % levels
        arrived = partner(window, "area", bit)
        start = delays[rnd, me_area] - steps
        used = lax.dynamic_slice_in_dim(arrived, start, steps, 0)
        panel = lax.all_gather(used, "neuron", axis=2, tiled=True)
        flat = panel.reshape(steps * batch, panel.shape[2] // block_side, block_side)
        picked = jnp.take(flat, block_index[rnd, 0], axis=1)
        contrib = jnp.einsum(
            "rjkc,jkcd->rjd", picked, weights[rnd, 0], preferred_element_type=jnp.float32
        )
        rec = rec + contrib.reshape(steps * batch, local_neurons)
    rec = rec.reshape(steps, batch, local_neurons)
    return adjoint_scan(err_grad, surrogate, rec, lv_end, la_end, alpha, rho, beta)


def solution(mesh):
    placed = (
        P(None, "groups", ("area", "neuron")),
        P(None, "groups", ("area", "neuron")),
        P(None, "groups", ("area", "neuron")),
        P("groups", ("area", "neuron")),
        P("groups", ("area", "neuron")),
        P(("area", "neuron")),
        P(("area", "neuron")),
        P(("area", "neuron")),
        P(None, "area", "neuron", None, None, None),
        P(None, "area", "neuron", None),
        P(),
    )
    return jax.shard_map(
        per_device,
        mesh=mesh,
        in_specs=placed,
        out_specs=(
            P(None, "groups", ("area", "neuron")),
            P("groups", ("area", "neuron")),
            P("groups", ("area", "neuron")),
        ),
        check_vma=False,
    )
```

profile of v0, /device:TPU:0, one launch (start us, length us, event | category | flops | bytes accessed | tf_op | source)
XLA Modules:
  0.0 206.2 jit_solution(3993261804340114842)
XLA Ops:
  7.2 3.1 %collective-permute-start = (bf16[32,8,2048]{2,1,0:T(8,128)(2,1)}, bf16[32,8,2048]{2,1,0:T(8,128)(2,1)S(1)}, u32[]{:S(2)}, u32[]{:S(2)}) collective-permute-start(bf16[32,8,2048]{2,1,0:T(8,128)(2,1)} %param.15), channel_id=1, source_target_pairs={{0,4},{4,0},{8,12},{12,8},{1,5},{5,1},{9,13},{13,9},{2,6},{6,2},{1... | collective-permute-start | bytes 3145736 | tf_op jit(solution)/shard_map/ppermute | solution.py:10
  10.3 1.5 constant_dynamic-slice_fusion.5
  14.4 19.3 %collective-permute-done = bf16[32,8,2048]{2,1,0:T(8,128)(2,1)S(1)} collective-permute-done((bf16[32,8,2048]{2,1,0:T(8,128)(2,1)}, bf16[32,8,2048]{2,1,0:T(8,128)(2,1)S(1)}, u32[]{:S(2)}, u32[]{:S(2)}) %collective-permute-start) | collective-permute-done | bytes 1048608 | tf_op jit(solution)/shard_map/ppermute | solution.py:10
  33.7 1.1 constant_dynamic-slice_fusion.1
  34.9 2.8 %collective-permute-start.1 = (bf16[32,8,2048]{2,1,0:T(8,128)(2,1)S(1)}, bf16[32,8,2048]{2,1,0:T(8,128)(2,1)S(1)}, u32[]{:S(2)}, u32[]{:S(2)}) collective-permute-start(bf16[32,8,2048]{2,1,0:T(8,128)(2,1)S(1)} %copy-done.12), channel_id=1, source_target_pairs={{0,8},{4,12},{8,0},{12,4},{1,9},{5,13},{9,1},{13,5},{2,10},{6,14},... | collective-permute-start | bytes 3145736 | tf_op jit(solution)/shard_map/ppermute | solution.py:10
  40.1 42.5 %collective-permute-done.1 = bf16[32,8,2048]{2,1,0:T(8,128)(2,1)S(1)} collective-permute-done((bf16[32,8,2048]{2,1,0:T(8,128)(2,1)S(1)}, bf16[32,8,2048]{2,1,0:T(8,128)(2,1)S(1)}, u32[]{:S(2)}, u32[]{:S(2)}) %collective-permute-start.1) | collective-permute-done | bytes 1048608 | tf_op jit(solution)/shard_map/ppermute | solution.py:10
  82.6 1.0 constant_dynamic-slice_fusion
  83.7 0.7 all-gather.9.cloned.1.call-update
  84.5 0.5 all-gather.11.cloned.1.call-update
  86.2 2.2 %copy.52 = bf16[16,8,64,128]{3,2,1,0:T(8,128)(2,1)S(1)} copy(bf16[16,8,64,128]{3,1,2,0:T(8,128)(2,1)} %bitcast.147) | data formatting | bytes 4194304
  88.4 1.4 copy.37
  89.8 17.6 %all-gather.7.cloned.1.call-done = bf16[16,8,8192]{2,1,0:T(8,128)(2,1)} async-done(((bf16[16,8,2048]{2,1,0:T(8,128)(2,1)}), bf16[16,8,8192]{2,1,0:T(8,128)(2,1)}) %all-gather.7.cloned.1.call-update) | async-done | bytes 2097168 | tf_op jit(solution)/shard_map/all_gather | solution.py:45
  107.4 2.2 %copy.53 = bf16[16,8,64,128]{3,2,1,0:T(8,128)(2,1)S(1)} copy(bf16[16,8,64,128]{3,1,2,0:T(8,128)(2,1)} %bitcast.148) | data formatting | bytes 4194304
  109.6 2.7 %copy.40 = bf16[128,64,128]{2,0,1:T(8,128)(2,1)} copy(bf16[128,64,128]{2,1,0:T(8,128)(2,1)S(1)} %bitcast.144) | data formatting | bytes 4194304 | tf_op jit(solution)/shard_map/reshape | solution.py:46
  112.3 19.9 %all-gather.9.cloned.1.call-done = bf16[16,8,8192]{2,1,0:T(8,128)(2,1)} async-done(((bf16[16,8,2048]{2,1,0:T(8,128)(2,1)}), bf16[16,8,8192]{2,1,0:T(8,128)(2,1)}) %all-gather.9.cloned.1.call-update) | async-done | bytes 2097168 | tf_op jit(solution)/shard_map/all_gather | solution.py:45
  132.2 2.2 %copy.54 = bf16[16,8,64,128]{3,2,1,0:T(8,128)(2,1)S(1)} copy(bf16[16,8,64,128]{3,1,2,0:T(8,128)(2,1)} %bitcast.149) | data formatting | bytes 4194304
  134.4 2.7 %copy.43 = bf16[128,64,128]{2,0,1:T(8,128)(2,1)} copy(bf16[128,64,128]{2,1,0:T(8,128)(2,1)S(1)} %bitcast.145) | data formatting | bytes 4194304 | tf_op jit(solution)/shard_map/reshape | solution.py:46
  137.1 19.1 %all-gather.11.cloned.1.call-done = bf16[16,8,8192]{2,1,0:T(8,128)(2,1)} async-done(((bf16[16,8,2048]{2,1,0:T(8,128)(2,1)}), bf16[16,8,8192]{2,1,0:T(8,128)(2,1)}) %all-gather.11.cloned.1.call-update) | async-done | bytes 2097168 | tf_op jit(solution)/shard_map/all_gather | solution.py:45
  156.2 2.2 %copy.55 = bf16[16,8,64,128]{3,2,1,0:T(8,128)(2,1)S(1)} copy(bf16[16,8,64,128]{3,1,2,0:T(8,128)(2,1)} %bitcast.150) | data formatting | bytes 4194304
  158.4 2.7 %copy.46 = bf16[128,64,128]{2,0,1:T(8,128)(2,1)} copy(bf16[128,64,128]{2,1,0:T(8,128)(2,1)S(1)} %bitcast.146) | data formatting | bytes 4194304 | tf_op jit(solution)/shard_map/reshape | solution.py:46
  161.1 2.1 %gather_fusion = bf16[64,128,128]{2,1,0:T(8,128)(2,1)} fusion(bf16[128,64,128]{2,0,1:T(8,128)(2,1)S(1)} %copy.37, s32[1024]{0:T(1024)S(1)} %pad_clamp_fusion.3), kind=kCustom, calls=%fused_computation.clone | custom fusion | bytes 4194560 | tf_op jit(solution)/shard_map/jit(_take)/gather | solution.py:47
  163.3 4.0 %gather_fusion.1 = bf16[64,128,128]{2,1,0:T(8,128)(2,1)} fusion(bf16[128,64,128]{2,0,1:T(8,128)(2,1)} %copy.40, s32[1024]{0:T(1024)S(1)} %pad_clamp_fusion.2), kind=kCustom, calls=%fused_computation.1.clone | custom fusion | bytes 4194560 | tf_op jit(solution)/shard_map/jit(_take)/gather | solution.py:47
  167.2 2.2 %gather_fusion.2 = bf16[64,128,128]{2,1,0:T(8,128)(2,1)} fusion(bf16[128,64,128]{2,0,1:T(8,128)(2,1)S(1)} %copy-done, s32[1024]{0:T(1024)S(1)} %pad_clamp_fusion.1), kind=kCustom, calls=%fused_computation.2.clone | custom fusion | bytes 4194560 | tf_op jit(solution)/shard_map/jit(_take)/gather | solution.py:47
  169.4 2.5 %gather_fusion.3 = bf16[64,128,128]{2,1,0:T(8,128)(2,1)S(1)} fusion(bf16[128,64,128]{2,0,1:T(8,128)(2,1)} %copy.46, s32[1024]{0:T(1024)S(1)} %pad_clamp_fusion), kind=kCustom, calls=%fused_computation.3.clone | custom fusion | bytes 4194560 | tf_op jit(solution)/shard_map/jit(_take)/gather | solution.py:47
  172.0 3.1 %fusion.28 = f32[16,128,128]{2,1,0:T(8,128)S(1)} fusion(bf16[4,1,16,4,128,128]{5,4,3,2,1,0:T(8,128)(2,1)} %param.23, bf16[16,4,128,128]{3,2,1,0:T(8,128)(2,1)} %bitcast.153, pred[16,4]{1,0:T(8,128)(4,1)S(1)} %copy.35), kind=kOutput, calls=%fused_computation.36 | convolution fusion | flops 269484032 | bytes 5242944 | tf_op jit(solution)/shard_map/rjkc,jkcd->rjd/dot_general | solution.py:48
  175.1 2.5 %fusion.63 = f32[16,128,128]{2,1,0:T(8,128)S(1)} fusion(f32[16,128,128]{2,1,0:T(8,128)S(1)} %fusion.28, bf16[4,1,16,4,128,128]{5,4,3,2,1,0:T(8,128)(2,1)} %param.23, bf16[16,4,128,128]{3,2,1,0:T(8,128)(2,1)S(1)} %bitcast.154, pred[16,4]{1,0:T(8,128)(4,1)S(1)} %copy.38), kind=kOutput, calls=%fused_computation.43 | convolution fusion | flops 269746176 | bytes 6291520 | tf_op jit(solution)/shard_map/rjkc,jkcd->rjd/dot_general | solution.py:48
  177.6 2.4 %fusion.58 = f32[16,128,128]{2,1,0:T(8,128)S(1)} fusion(f32[16,128,128]{2,1,0:T(8,128)S(1)} %fusion.63, bf16[4,1,16,4,128,128]{5,4,3,2,1,0:T(8,128)(2,1)} %param.23, bf16[16,4,128,128]{3,2,1,0:T(8,128)(2,1)S(1)} %bitcast.152, pred[16,4]{1,0:T(8,128)(4,1)S(1)} %copy.41), kind=kOutput, calls=%fused_computation.42 | convolution fusion | flops 269746176 | bytes 6291520 | tf_op jit(solution)/shard_map/rjkc,jkcd->rjd/dot_general | solution.py:48
  180.0 2.4 %fusion.53 = f32[128,16,128]{2,0,1:T(8,128)S(1)} fusion(f32[16,128,128]{2,1,0:T(8,128)S(1)} %fusion.58, bf16[4,1,16,4,128,128]{5,4,3,2,1,0:T(8,128)(2,1)} %param.23, bf16[16,4,128,128]{3,2,1,0:T(8,128)(2,1)S(1)} %bitcast.151, pred[16,4]{1,0:T(8,128)(4,1)S(1)} %copy.44), kind=kOutput, calls=%fused_computation.41 | convolution fusion | flops 269746176 | bytes 6291520 | tf_op jit(solution)/shard_map/rjkc,jkcd->rjd/dot_general | solution.py:48
  182.5 0.6 copy.47
  183.4 15.5 %while.18 = (s32[]{:T(128)}, f32[8,2048]{1,0:T(8,128)S(1)}, f32[8,2048]{1,0:T(8,128)S(1)}, bf16[16,8,2048]{2,1,0:T(8,128)(2,1)S(1)}, f32[2048]{0:T(1024)S(1)}, /...) while((s32[]{:T(128)}, f32[8,2048]{1,0:T(8,128)S(1)}, ...), condition=%wide.region_1.3_spmd, body=%wide.region_0.0_spmd.sunk | while | flops 180227 | bytes 581769 | solution.py:23
  183.4 0.9 fusion.77
  184.4 0.9 fusion.77
  185.3 0.9 fusion.77
  186.3 0.9 fusion.77
  187.3 0.9 fusion.77
  188.2 0.9 fusion.77
  189.2 0.9 fusion.77
  190.2 0.9 fusion.77
  191.1 0.9 fusion.77
  192.1 0.9 fusion.77
  193.1 0.9 fusion.77
  194.0 0.9 fusion.77
  195.0 0.9 fusion.77
  196.0 0.9 fusion.77
  196.9 0.9 fusion.77
  197.9 0.9 fusion.77
  198.9 0.6 copy-done.1
  199.5 0.2 copy-done.7
  (67 shorter events, 1.8 us)
Async XLA Ops:
  7.2 27.7 %copy-start.12 = (bf16[32,8,2048]{2,1,0:T(8,128)(2,1)S(1)}, bf16[32,8,2048]{2,1,0:T(8,128)(2,1)}, u32[]{:S(2)}) copy-start(bf16[32,8,2048]{2,1,0:T(8,128)(2,1)} %param.15) | copy-start | bytes 3145732
  7.2 79.0 %all-gather.5.cloned.1.call-start = ((), (), s32[]{:S(2)}) async-start(), calls=%async_computation | async-start | bytes 2621440 | tf_op jit(solution)/shard_map/all_gather | solution.py:45
  7.2 26.5 %collective-permute-start = (bf16[32,8,2048]{2,1,0:T(8,128)(2,1)}, bf16[32,8,2048]{2,1,0:T(8,128)(2,1)S(1)}, u32[]{:S(2)}, u32[]{:S(2)}) collective-permute-start(bf16[32,8,2048]{2,1,0:T(8,128)(2,1)} %param.15), channel_id=1, source_target_pairs={{0,4},{4,0},{8,12},{12,8},{1,5},{5,1},{9,13},{13,9},{2,6},{6,2},{1... | collective-permute-start | bytes 3145736 | tf_op jit(solution)/shard_map/ppermute | solution.py:10
  34.8 50.2 %copy-start.11 = (s32[4,1,16,4]{2,3,1,0:T(4,128)S(1)}, s32[4,1,16,4]{2,3,1,0:T(4,128)}, u32[]{:S(2)}) copy-start(s32[4,1,16,4]{2,3,1,0:T(4,128)} %param.24) | copy-start | bytes 3076
  34.8 72.6 %all-gather.7.cloned.1.call-start = ((), (), s32[]{:S(2)}) async-start(), calls=%async_computation.1 | async-start | bytes 2621440 | tf_op jit(solution)/shard_map/all_gather | solution.py:45
  34.9 47.8 %collective-permute-start.1 = (bf16[32,8,2048]{2,1,0:T(8,128)(2,1)S(1)}, bf16[32,8,2048]{2,1,0:T(8,128)(2,1)S(1)}, u32[]{:S(2)}, u32[]{:S(2)}) collective-permute-start(bf16[32,8,2048]{2,1,0:T(8,128)(2,1)S(1)} %copy-done.12), channel_id=1, source_target_pairs={{0,8},{4,12},{8,0},{12,4},{1,9},{5,13},{9,1},{13,5},{2,10},{6,14},... | collective-permute-start | bytes 3145736 | tf_op jit(solution)/shard_map/ppermute | solution.py:10
  83.7 48.5 %all-gather.9.cloned.1.call-start = ((), (), s32[]{:S(2)}) async-start(), calls=%async_computation.2 | async-start | bytes 2621440 | tf_op jit(solution)/shard_map/all_gather | solution.py:45
  84.4 71.8 %all-gather.11.cloned.1.call-start = ((), (), s32[]{:S(2)}) async-start(), calls=%async_computation.3 | async-start | bytes 2621440 | tf_op jit(solution)/shard_map/all_gather | solution.py:45
  163.3 4.0 %copy-start = (bf16[128,64,128]{2,0,1:T(8,128)(2,1)S(1)}, bf16[128,64,128]{2,0,1:T(8,128)(2,1)}, u32[]{:S(2)}) copy-start(bf16[128,64,128]{2,0,1:T(8,128)(2,1)} %copy.43) | copy-start | bytes 6291460
  171.9 3.1 %copy-start.6 = (bf16[64,128,128]{2,1,0:T(8,128)(2,1)S(1)}, bf16[64,128,128]{2,1,0:T(8,128)(2,1)}, u32[]{:S(2)}) copy-start(bf16[64,128,128]{2,1,0:T(8,128)(2,1)} %gather_fusion.1) | copy-start | bytes 6291460
  175.1 2.6 %copy-start.5 = (bf16[64,128,128]{2,1,0:T(8,128)(2,1)S(1)}, bf16[64,128,128]{2,1,0:T(8,128)(2,1)}, u32[]{:S(2)}) copy-start(bf16[64,128,128]{2,1,0:T(8,128)(2,1)} %gather_fusion.2) | copy-start | bytes 6291460
  182.4 0.9 copy-start.2
  182.5 0.9 copy-start.4
  182.5 0.9 copy-start.8
  182.5 0.9 copy-start.9
  182.5 0.9 copy-start.10
  198.8 0.6 copy-start.1
  198.9 0.6 copy-start.3
  198.9 0.8 copy-start.7
Sparse Core Ops, SparseCore 0:
  34.9 23.9 all-gather.4
  83.8 23.5 all-gather.6
  109.6 22.5 all-gather.8
  133.6 22.5 all-gather.10
where the time goes:
time: 207 us; the launch traced here: 206 us
  waiting for transfers between devices  120 us (58%)
  local copies, waits for them, and re-layouts  35.4 us (17%)
  between operations  19.1 us (9%)
  other arithmetic  15.2 us (7%)
  matrix products  10.4 us (5%)
  starting transfers between devices  6.07 us (3%)
    ppermute x2, waiting for transfers between devices, partner(): return lax.ppermute(value, axis, pairs)  61.8 us
    all_gather x4, waiting for transfers between devices, per_device(): panel = lax.all_gather(used, 'neuron', axis=2, tiled=True)  56.6 us
    sub x16, other arithmetic, step(): la_next = rho * la_now - beta * surr_t * total  15 us
    gather x4, local copies, waits for them, and re-layouts, per_device(): picked = jnp.take(flat, block_index[rnd, 0], axis=1)  10.8 us
    dot_general x4, matrix products, per_device(): jnp.einsum('rjkc,jkcd->rjd', picked, weights[rnd, 0], preferred_element_t...  10.4 us
    unnamed x30, local copies, waits for them, and re-layouts  9.6 us
    reshape x4, local copies, waits for them, and re-layouts, per_device(): panel.reshape(steps * batch, panel.shape[2] // block_side, block_side)  9.53 us
    ppermute x2, starting transfers between devices, partner(): return lax.ppermute(value, axis, pairs)  5.91 us
  transfers between devices with their start and end apart: 6, of which 5 were waited for; matrix products, arithmetic and copies ran while one was open for 8% of the time, Pallas kernels for 0%

commit v1 on v0

--- a/solution.py
+++ b/solution.py
@@ -2,6 +2,27 @@
 import jax.numpy as jnp
 from jax import lax
 from jax.sharding import PartitionSpec as P
+
+
+def in_order(pieces, dim):
+    dims = list(pieces.shape[1:])
+    dims[dim] *= pieces.shape[0]
+    return jnp.moveaxis(pieces, 0, dim).reshape(dims)
+
+
+def collected_by_bits(array, axis):
+    size, mine = (lax.axis_size(axis), lax.axis_index(axis))
+    tiles, bit = (array[None], 1)
+    while bit < size:
+        received = lax.ppermute(tiles, axis, [(i, i ^ bit) for i in range(size)])
+        low = mine & bit == 0
+        tiles = jnp.concatenate([jnp.where(low, tiles, received), jnp.where(low, received, tiles)])
+        bit *= 2
+    return tiles
+
+
+def gather_by_bits(x, axis, dim):
+    return in_order(collected_by_bits(x, axis), dim)
 
 
 def partner(value, axis, bit):
@@ -42,7 +63,7 @@
         arrived = partner(window, "area", bit)
         start = delays[rnd, me_area] - steps
         used = lax.dynamic_slice_in_dim(arrived, start, steps, 0)
-        panel = lax.all_gather(used, "neuron", axis=2, tiled=True)
+        panel = gather_by_bits(used, "neuron", 2)
         flat = panel.reshape(steps * batch, panel.shape[2] // block_side, block_side)
         picked = jnp.take(flat, block_index[rnd, 0], axis=1)
         contrib = jnp.einsum(

time: 207 us -> 217 us (1.048)
  local copies, waits for them, and re-layouts: 35.4 us -> 60.7 us
  waiting for transfers between devices: 120 us -> 102 us
  between operations: 19.1 us -> 6.08 us
  other arithmetic: 15.2 us -> 24.9 us
  starting transfers between devices: 6.07 us -> 11.3 us
    ppermute x0 -> x8, waiting for transfers between devices: none -> 63.2 us  [collected_by_bits(): received = lax.ppermute(tiles, axis, [(i, i ^ bit) for i in range(size)])]
    all_gather x4 -> x0, waiting for transfers between devices: 56.6 us -> none  [per_device(): panel = lax.all_gather(used, 'neuron', axis=2, tiled=True)]
    another operation x0 -> x8, local copies, waits for them, and re-layouts: none -> 32.3 us  [per_device(): panel.reshape(steps * batch, panel.shape[2] // block_side, block_side)]
    ppermute x2, waiting for transfers between devices: 61.8 us -> 38.5 us  [partner(): return lax.ppermute(value, axis, pairs)]
    transpose x0 -> x4, local copies, waits for them, and re-layouts: none -> 11.1 us  [in_order(): return jnp.moveaxis(pieces, 0, dim).reshape(dims)]
    reshape x4 -> x0, local copies, waits for them, and re-layouts: 9.53 us -> none  [per_device(): panel.reshape(steps * batch, panel.shape[2] // block_side, block_side)]
    unnamed x30 -> x38, local copies, waits for them, and re-layouts: 9.6 us -> 1.7 us
    ppermute x0 -> x8, starting transfers between devices: none -> 5.62 us  [collected_by_bits(): received = lax.ppermute(tiles, axis, [(i, i ^ bit) for i in range(size)])]
  transfers between devices with their start and end apart: 6 -> 10, of which waited for: 5 -> 5; matrix products, arithmetic and copies ran while one was open for 8% -> 14% of each run, Pallas kernels for 0% -> 0%
where the time goes in v1:
time: 217 us; the launch traced here: 216 us
  waiting for transfers between devices  102 us (47%)
  local copies, waits for them, and re-layouts  60.7 us (28%)
  other arithmetic  24.9 us (11%)
  starting transfers between devices  11.3 us (5%)
  matrix products  10.4 us (5%)
  between operations  6.08 us (3%)
    ppermute x8, waiting for transfers between devices, collected_by_bits(): received = lax.ppermute(tiles, axis, [(i, i ^ bit) for i in range(size)])  63.2 us
    ppermute x2, waiting for transfers between devices, partner(): return lax.ppermute(value, axis, pairs)  38.5 us
    another operation x8, local copies, waits for them, and re-layouts, per_device(): panel.reshape(steps * batch, panel.shape[2] // block_side, block_side)  32.3 us
    sub x16, other arithmetic, step(): la_next = rho * la_now - beta * surr_t * total  15 us
    transpose x4, local copies, waits for them, and re-layouts, in_order(): return jnp.moveaxis(pieces, 0, dim).reshape(dims)  11.1 us
    gather x4, local copies, waits for them, and re-layouts, per_device(): picked = jnp.take(flat, block_index[rnd, 0], axis=1)  10.9 us
    dot_general x4, matrix products, per_device(): jnp.einsum('rjkc,jkcd->rjd', picked, weights[rnd, 0], preferred_element_t...  10.4 us
    ppermute x2, starting transfers between devices, partner(): return lax.ppermute(value, axis, pairs)  5.68 us
  transfers between devices with their start and end apart: 10, of which 5 were waited for; matrix products, arithmetic and copies ran while one was open for 14% of the time, Pallas kernels for 0%

profile of v1, /device:TPU:0, one launch (start us, length us, event | category | flops | bytes accessed | tf_op | source)
XLA Modules:
  0.0 215.5 jit_solution(8594273243336271734)
XLA Ops:
  0.6 4.1 %collective-permute-start.3 = (bf16[32,8,2048]{2,1,0:T(8,128)(2,1)}, bf16[32,8,2048]{2,1,0:T(8,128)(2,1)}, u32[]{:S(2)}, u32[]{:S(2)}) collective-permute-start(bf16[32,8,2048]{2,1,0:T(8,128)(2,1)} %param.15), channel_id=1, source_target_pairs={{0,8},{4,12},{8,0},{12,4},{1,9},{5,13},{9,1},{13,5},{2,10},{6,14},... | collective-permute-start | bytes 3145736 | tf_op jit(solution)/shard_map/ppermute | solution.py:31
  4.7 1.6 collective-permute-start
  6.3 1.5 constant_dynamic-slice_fusion.1
  12.2 38.5 %collective-permute-done.3 = bf16[32,8,2048]{2,1,0:T(8,128)(2,1)} collective-permute-done((bf16[32,8,2048]{2,1,0:T(8,128)(2,1)}, bf16[32,8,2048]{2,1,0:T(8,128)(2,1)}, u32[]{:S(2)}, u32[]{:S(2)}) %collective-permute-start.3) | collective-permute-done | bytes 1048608 | tf_op jit(solution)/shard_map/ppermute | solution.py:31
  50.8 1.3 dynamic-slice_bitcast_fusion
  56.8 1.6 collective-permute-start.5
  59.5 1.1 pad_maximum_fusion.3
  60.5 1.2 collective-permute-start.9
  62.7 1.2 pad_maximum_fusion.2
  64.7 18.2 %collective-permute-done.5 = bf16[2,16,8,2048]{3,2,1,0:T(8,128)(2,1)S(1)} collective-permute-done((bf16[2,16,8,2048]{3,2,1,0:T(8,128)(2,1)S(1)}, bf16[2,16,8,2048]{3,2,1,0:T(8,128)(2,1)S(1)}, u32[]{:S(2)}, u32[]{:S(2)}) %collective-permute-start.5) | collective-permute-done | bytes 1048608 | tf_op jit(solution)/shard_map/ppermute | solution.py:17
  82.8 22.5 %collective-permute-done.2 = bf16[2,16,8,2048]{3,2,1,0:T(8,128)(2,1)S(1)} collective-permute-done((bf16[2,16,8,2048]{3,2,1,0:T(8,128)(2,1)S(1)}, bf16[2,16,8,2048]{3,2,1,0:T(8,128)(2,1)S(1)}, u32[]{:S(2)}, u32[]{:S(2)}) %collective-permute-start.2) | collective-permute-done | bytes 1048608 | tf_op jit(solution)/shard_map/ppermute | solution.py:17
  105.3 1.6 broadcast_select_fusion.5
  107.1 1.8 copy.36
  108.9 2.8 %reshape_reshape.12 = bf16[128,64,128]{2,1,0:T(8,128)(2,1)} reshape(bf16[16,8,4,2048]{3,2,1,0:T(4,128)(2,1)S(1)} %copy.36) | data formatting | bytes 4194304 | tf_op jit(solution)/shard_map/reshape;reshape | solution.py:67
  111.7 3.1 %copy.38 = bf16[128,64,128]{2,0,1:T(8,128)(2,1)S(1)} copy(bf16[128,64,128]{2,1,0:T(8,128)(2,1)} %reshape_reshape.12) | data formatting | bytes 4194304 | tf_op jit(solution)/shard_map/reshape;reshape | solution.py:67
  115.0 3.1 %copy.40 = bf16[16,8,4,2048]{3,2,1,0:T(4,128)(2,1)} copy(bf16[16,8,4,2048]{3,1,0,2:T(8,128)(2,1)S(1)} %maximum_bitcast_fusion.1) | data formatting | bytes 4194304 | tf_op jit(solution)/shard_map/transpose | solution.py:10
  118.2 4.4 %reshape_reshape.13 = bf16[128,64,128]{2,1,0:T(8,128)(2,1)} reshape(bf16[16,8,4,2048]{3,2,1,0:T(4,128)(2,1)} %copy.40) | data formatting | bytes 4194304 | tf_op jit(solution)/shard_map/reshape;reshape | solution.py:67
  122.5 4.4 %copy.42 = bf16[128,64,128]{2,0,1:T(8,128)(2,1)} copy(bf16[128,64,128]{2,1,0:T(8,128)(2,1)} %reshape_reshape.13) | data formatting | bytes 4194304 | tf_op jit(solution)/shard_map/reshape;reshape | solution.py:67
  126.9 0.9 collective-permute-done.9
  127.9 21.6 %collective-permute-done.7 = bf16[2,16,8,2048]{3,2,1,0:T(8,128)(2,1)} collective-permute-done((bf16[2,16,8,2048]{3,2,1,0:T(8,128)(2,1)}, bf16[2,16,8,2048]{3,2,1,0:T(8,128)(2,1)}, u32[]{:S(2)}, u32[]{:S(2)}) %collective-permute-start.7) | collective-permute-done | bytes 1048608 | tf_op jit(solution)/shard_map/ppermute | solution.py:17
  149.5 3.2 %broadcast_select_fusion.1 = (bf16[2,16,8,2048]{3,2,1,0:T(8,128)(2,1)}, bf16[2,16,8,2048]{3,2,1,0:T(8,128)(2,1)}, bf16[2,16,8,2048]{3,2,1,0:T(8,128)(2,1)S(1)}, bf16[2,16,8,2048]{3,2,1,0:T(8,128)(2,1)S(1)}) fusion(bf16[2,16,8,2048]{3,2,1,0:T(8,128)(2,1)} %collective-permute-done.9, pred[]{:T(512)S(6)} %eq.4, ...), kind=kLoop, calls=%fused_computation.57 | loop fusion | flops 3145728 | bytes 8388609 | tf_op jit(solution)/shard_map/jit(_where)/select_n | solution.py:19
  152.9 3.1 %copy.44 = bf16[16,8,4,2048]{3,2,1,0:T(4,128)(2,1)} copy(bf16[16,8,4,2048]{3,1,0,2:T(8,128)(2,1)S(1)} %maximum_bitcast_fusion.2) | data formatting | bytes 4194304 | tf_op jit(solution)/shard_map/transpose | solution.py:10
  156.0 4.4 %reshape_reshape.14 = bf16[128,64,128]{2,1,0:T(8,128)(2,1)} reshape(bf16[16,8,4,2048]{3,2,1,0:T(4,128)(2,1)} %copy.44) | data formatting | bytes 4194304 | tf_op jit(solution)/shard_map/reshape;reshape | solution.py:67
  160.4 4.4 %copy.46 = bf16[128,64,128]{2,0,1:T(8,128)(2,1)} copy(bf16[128,64,128]{2,1,0:T(8,128)(2,1)} %reshape_reshape.14) | data formatting | bytes 4194304 | tf_op jit(solution)/shard_map/reshape;reshape | solution.py:67
  165.0 3.1 %copy.48 = bf16[16,8,4,2048]{3,2,1,0:T(4,128)(2,1)} copy(bf16[16,8,4,2048]{3,1,0,2:T(8,128)(2,1)S(1)} %maximum_bitcast_fusion.3) | data formatting | bytes 4194304 | tf_op jit(solution)/shard_map/transpose | solution.py:10
  168.2 4.4 %reshape_reshape.15 = bf16[128,64,128]{2,1,0:T(8,128)(2,1)} reshape(bf16[16,8,4,2048]{3,2,1,0:T(4,128)(2,1)} %copy.48) | data formatting | bytes 4194304 | tf_op jit(solution)/shard_map/reshape;reshape | solution.py:67
  172.6 4.3 %copy.50 = bf16[128,64,128]{2,0,1:T(8,128)(2,1)} copy(bf16[128,64,128]{2,1,0:T(8,128)(2,1)} %reshape_reshape.15) | data formatting | bytes 4194304 | tf_op jit(solution)/shard_map/reshape;reshape | solution.py:67
  176.9 2.2 %gather_fusion = bf16[64,128,128]{2,1,0:T(8,128)(2,1)} fusion(bf16[128,64,128]{2,0,1:T(8,128)(2,1)S(1)} %copy.38, s32[1024]{0:T(1024)S(1)} %pad_clamp_fusion.3), kind=kCustom, calls=%fused_computation.clone | custom fusion | bytes 4194560 | tf_op jit(solution)/shard_map/jit(_take)/gather | solution.py:68
  179.1 3.9 %gather_fusion.1 = bf16[64,128,128]{2,1,0:T(8,128)(2,1)} fusion(bf16[128,64,128]{2,0,1:T(8,128)(2,1)} %copy.42, s32[1024]{0:T(1024)S(1)} %pad_clamp_fusion.2), kind=kCustom, calls=%fused_computation.1.clone | custom fusion | bytes 4194560 | tf_op jit(solution)/shard_map/jit(_take)/gather | solution.py:68
  183.1 2.2 %gather_fusion.2 = bf16[64,128,128]{2,1,0:T(8,128)(2,1)} fusion(bf16[128,64,128]{2,0,1:T(8,128)(2,1)S(1)} %copy-done, s32[1024]{0:T(1024)S(1)} %pad_clamp_fusion.1), kind=kCustom, calls=%fused_computation.2.clone | custom fusion | bytes 4194560 | tf_op jit(solution)/shard_map/jit(_take)/gather | solution.py:68
  185.2 2.5 %gather_fusion.3 = bf16[64,128,128]{2,1,0:T(8,128)(2,1)S(1)} fusion(bf16[128,64,128]{2,0,1:T(8,128)(2,1)} %copy.50, s32[1024]{0:T(1024)S(1)} %pad_clamp_fusion), kind=kCustom, calls=%fused_computation.3.clone | custom fusion | bytes 4194560 | tf_op jit(solution)/shard_map/jit(_take)/gather | solution.py:68
  187.8 3.1 %fusion.28 = f32[16,128,128]{2,1,0:T(8,128)S(1)} fusion(bf16[4,1,16,4,128,128]{5,4,3,2,1,0:T(8,128)(2,1)} %param.23, bf16[16,4,128,128]{3,2,1,0:T(8,128)(2,1)} %bitcast.149, pred[16,4]{1,0:T(8,128)(4,1)S(1)} %copy.35), kind=kOutput, calls=%fused_computation.40 | convolution fusion | flops 269484032 | bytes 5242944 | tf_op jit(solution)/shard_map/rjkc,jkcd->rjd/dot_general | solution.py:69
  190.9 2.5 %fusion.63 = f32[16,128,128]{2,1,0:T(8,128)S(1)} fusion(f32[16,128,128]{2,1,0:T(8,128)S(1)} %fusion.28, bf16[4,1,16,4,128,128]{5,4,3,2,1,0:T(8,128)(2,1)} %param.23, bf16[16,4,128,128]{3,2,1,0:T(8,128)(2,1)S(1)} %bitcast.150, pred[16,4]{1,0:T(8,128)(4,1)S(1)} %copy.39), kind=kOutput, calls=%fused_computation.47 | convolution fusion | flops 269746176 | bytes 6291520 | tf_op jit(solution)/shard_map/rjkc,jkcd->rjd/dot_general | solution.py:69
  193.5 2.4 %fusion.58 = f32[16,128,128]{2,1,0:T(8,128)S(1)} fusion(f32[16,128,128]{2,1,0:T(8,128)S(1)} %fusion.63, bf16[4,1,16,4,128,128]{5,4,3,2,1,0:T(8,128)(2,1)} %param.23, bf16[16,4,128,128]{3,2,1,0:T(8,128)(2,1)S(1)} %bitcast.148, pred[16,4]{1,0:T(8,128)(4,1)S(1)} %copy.43), kind=kOutput, calls=%fused_computation.46 | convolution fusion | flops 269746176 | bytes 6291520 | tf_op jit(solution)/shard_map/rjkc,jkcd->rjd/dot_general | solution.py:69
  195.9 2.4 %fusion.53 = f32[128,16,128]{2,0,1:T(8,128)S(1)} fusion(f32[16,128,128]{2,1,0:T(8,128)S(1)} %fusion.58, bf16[4,1,16,4,128,128]{5,4,3,2,1,0:T(8,128)(2,1)} %param.23, bf16[16,4,128,128]{3,2,1,0:T(8,128)(2,1)S(1)} %bitcast.147, pred[16,4]{1,0:T(8,128)(4,1)S(1)} %copy.47), kind=kOutput, calls=%fused_computation.45 | convolution fusion | flops 269746176 | bytes 6291520 | tf_op jit(solution)/shard_map/rjkc,jkcd->rjd/dot_general | solution.py:69
  199.2 15.5 %while.18 = (s32[]{:T(128)}, f32[8,2048]{1,0:T(8,128)S(1)}, f32[8,2048]{1,0:T(8,128)S(1)}, bf16[16,8,2048]{2,1,0:T(8,128)(2,1)S(1)}, f32[2048]{0:T(1024)S(1)}, /...) while((s32[]{:T(128)}, f32[8,2048]{1,0:T(8,128)S(1)}, ...), condition=%wide.region_1.3_spmd, body=%wide.region_0.2_spmd.sunk | while | flops 180227 | bytes 581777 | solution.py:44
  199.2 0.9 fusion.77
  200.2 0.9 fusion.77
  201.2 0.9 fusion.77
  202.1 0.9 fusion.77
  203.1 0.9 fusion.77
  204.1 0.9 fusion.77
  205.0 0.9 fusion.77
  206.0 0.9 fusion.77
  207.9 0.9 fusion.77
  209.9 0.9 fusion.77
  211.8 0.9 fusion.77
  213.7 0.9 fusion.77
  (101 shorter events, 13.1 us)
Async XLA Ops:
  0.6 50.2 %collective-permute-start.3 = (bf16[32,8,2048]{2,1,0:T(8,128)(2,1)}, bf16[32,8,2048]{2,1,0:T(8,128)(2,1)}, u32[]{:S(2)}, u32[]{:S(2)}) collective-permute-start(bf16[32,8,2048]{2,1,0:T(8,128)(2,1)} %param.15), channel_id=1, source_target_pairs={{0,8},{4,12},{8,0},{12,4},{1,9},{5,13},{9,1},{13,5},{2,10},{6,14},... | collective-permute-start | bytes 3145736 | tf_op jit(solution)/shard_map/ppermute | solution.py:31
  4.7 50.6 %collective-permute-start = (bf16[32,8,2048]{2,1,0:T(8,128)(2,1)}, bf16[32,8,2048]{2,1,0:T(8,128)(2,1)S(1)}, u32[]{:S(2)}, u32[]{:S(2)}) collective-permute-start(bf16[32,8,2048]{2,1,0:T(8,128)(2,1)} %param.15), channel_id=1, source_target_pairs={{0,4},{4,0},{8,12},{12,8},{1,5},{5,1},{9,13},{13,9},{2,6},{6,2},{1... | collective-permute-start | bytes 3145736 | tf_op jit(solution)/shard_map/ppermute | solution.py:31
  52.1 4.5 %collective-permute-start.4 = (bf16[1,16,8,2048]{3,2,1,0:T(8,128)(2,1)S(1)}, bf16[1,16,8,2048]{3,2,1,0:T(8,128)(2,1)S(1)}, u32[]{:S(2)}, u32[]{:S(2)}) collective-permute-start(bf16[1,16,8,2048]{3,2,1,0:T(8,128)(2,1)S(1)} %get-tuple-element.240), channel_id=1, source_target_pairs={{0,1},{1,0},{2,3},{3,2},{4,5},{5,4},{6,7},{7,6},{8,9},{9,8},{10,11... | collective-permute-start | bytes 1572872 | tf_op jit(solution)/shard_map/ppermute | solution.py:17
  55.5 2.9 %collective-permute-start.1 = (bf16[1,16,8,2048]{3,2,1,0:T(8,128)(2,1)S(1)}, bf16[1,16,8,2048]{3,2,1,0:T(8,128)(2,1)S(1)}, u32[]{:S(2)}, u32[]{:S(2)}) collective-permute-start(bf16[1,16,8,2048]{3,2,1,0:T(8,128)(2,1)S(1)} %get-tuple-element.244), channel_id=1, source_target_pairs={{0,1},{1,0},{2,3},{3,2},{4,5},{5,4},{6,7},{7,6},{8,9},{9,8},{10,11... | collective-permute-start | bytes 1572872 | tf_op jit(solution)/shard_map/ppermute | solution.py:17
  56.1 3.3 %collective-permute-start.8 = (bf16[1,16,8,2048]{3,2,1,0:T(8,128)(2,1)S(1)}, bf16[1,16,8,2048]{3,2,1,0:T(8,128)(2,1)S(1)}, u32[]{:S(2)}, u32[]{:S(2)}) collective-permute-start(bf16[1,16,8,2048]{3,2,1,0:T(8,128)(2,1)S(1)} %get-tuple-element.239), channel_id=1, source_target_pairs={{0,1},{1,0},{2,3},{3,2},{4,5},{5,4},{6,7},{7,6},{8,9},{9,8},{10,11... | collective-permute-start | bytes 1572872 | tf_op jit(solution)/shard_map/ppermute | solution.py:17
  56.1 5.6 %collective-permute-start.6 = (bf16[1,16,8,2048]{3,2,1,0:T(8,128)(2,1)S(1)}, bf16[1,16,8,2048]{3,2,1,0:T(8,128)(2,1)S(1)}, u32[]{:S(2)}, u32[]{:S(2)}) collective-permute-start(bf16[1,16,8,2048]{3,2,1,0:T(8,128)(2,1)S(1)} %get-tuple-element.243), channel_id=1, source_target_pairs={{0,1},{1,0},{2,3},{3,2},{4,5},{5,4},{6,7},{7,6},{8,9},{9,8},{10,11... | collective-permute-start | bytes 1572872 | tf_op jit(solution)/shard_map/ppermute | solution.py:17
  56.8 26.1 %collective-permute-start.5 = (bf16[2,16,8,2048]{3,2,1,0:T(8,128)(2,1)S(1)}, bf16[2,16,8,2048]{3,2,1,0:T(8,128)(2,1)S(1)}, u32[]{:S(2)}, u32[]{:S(2)}) collective-permute-start(bf16[2,16,8,2048]{3,2,1,0:T(8,128)(2,1)S(1)} %pad_maximum_fusion.1), channel_id=1, source_target_pairs={{0,2},{1,3},{2,0},{3,1},{4,6},{5,7},{6,4},{7,5},{8,10},{9,11},{10,... | collective-permute-start | bytes 3145736 | tf_op jit(solution)/shard_map/ppermute | solution.py:17
  58.5 46.8 %collective-permute-start.2 = (bf16[2,16,8,2048]{3,2,1,0:T(8,128)(2,1)S(1)}, bf16[2,16,8,2048]{3,2,1,0:T(8,128)(2,1)S(1)}, u32[]{:S(2)}, u32[]{:S(2)}) collective-permute-start(bf16[2,16,8,2048]{3,2,1,0:T(8,128)(2,1)S(1)} %pad_maximum_fusion), channel_id=1, source_target_pairs={{0,2},{1,3},{2,0},{3,1},{4,6},{5,7},{6,4},{7,5},{8,10},{9,11},{10,... | collective-permute-start | bytes 3145736 | tf_op jit(solution)/shard_map/ppermute | solution.py:17
  60.5 67.3 %collective-permute-start.9 = (bf16[2,16,8,2048]{3,2,1,0:T(8,128)(2,1)}, bf16[2,16,8,2048]{3,2,1,0:T(8,128)(2,1)}, u32[]{:S(2)}, u32[]{:S(2)}) collective-permute-start(bf16[2,16,8,2048]{3,2,1,0:T(8,128)(2,1)} %pad_maximum_fusion.3), channel_id=1, source_target_pairs={{0,2},{1,3},{2,0},{3,1},{4,6},{5,7},{6,4},{7,5},{8,10},{9,11},{10,... | collective-permute-start | bytes 3145736 | tf_op jit(solution)/shard_map/ppermute | solution.py:17
  61.9 0.8 copy-start.3
  61.9 2.0 copy-start.5
  63.9 85.6 %collective-permute-start.7 = (bf16[2,16,8,2048]{3,2,1,0:T(8,128)(2,1)}, bf16[2,16,8,2048]{3,2,1,0:T(8,128)(2,1)}, u32[]{:S(2)}, u32[]{:S(2)}) collective-permute-start(bf16[2,16,8,2048]{3,2,1,0:T(8,128)(2,1)} %pad_maximum_fusion.2), channel_id=1, source_target_pairs={{0,2},{1,3},{2,0},{3,1},{4,6},{5,7},{6,4},{7,5},{8,10},{9,11},{10,... | collective-permute-start | bytes 3145736 | tf_op jit(solution)/shard_map/ppermute | solution.py:17
  111.7 3.1 %copy-start.9 = (bf16[2,16,8,2048]{3,2,1,0:T(8,128)(2,1)S(1)}, bf16[2,16,8,2048]{3,2,1,0:T(8,128)(2,1)}, u32[]{:S(2)}) copy-start(bf16[2,16,8,2048]{3,2,1,0:T(8,128)(2,1)} %get-tuple-element.233) | copy-start | bytes 3145732
  111.7 3.1 %copy-start.10 = (bf16[2,16,8,2048]{3,2,1,0:T(8,128)(2,1)S(1)}, bf16[2,16,8,2048]{3,2,1,0:T(8,128)(2,1)}, u32[]{:S(2)}) copy-start(bf16[2,16,8,2048]{3,2,1,0:T(8,128)(2,1)} %get-tuple-element.234) | copy-start | bytes 3145732
  122.5 26.9 %copy-start.4 = (bf16[1,16,8,2048]{3,2,1,0:T(8,128)(2,1)S(1)}, bf16[1,16,8,2048]{3,2,1,0:T(8,128)(2,1)}, u32[]{:S(2)}) copy-start(bf16[1,16,8,2048]{3,2,1,0:T(8,128)(2,1)} %copy-done.3) | copy-start | bytes 1572868
  122.5 26.9 %copy-start.6 = (bf16[1,16,8,2048]{3,2,1,0:T(8,128)(2,1)S(1)}, bf16[1,16,8,2048]{3,2,1,0:T(8,128)(2,1)}, u32[]{:S(2)}) copy-start(bf16[1,16,8,2048]{3,2,1,0:T(8,128)(2,1)} %copy-done.5) | copy-start | bytes 1572868
  160.4 4.4 %copy-start.7 = (bf16[2,16,8,2048]{3,2,1,0:T(8,128)(2,1)S(1)}, bf16[2,16,8,2048]{3,2,1,0:T(8,128)(2,1)}, u32[]{:S(2)}) copy-start(bf16[2,16,8,2048]{3,2,1,0:T(8,128)(2,1)} %get-tuple-element.229) | copy-start | bytes 3145732
  160.4 4.4 %copy-start.8 = (bf16[2,16,8,2048]{3,2,1,0:T(8,128)(2,1)S(1)}, bf16[2,16,8,2048]{3,2,1,0:T(8,128)(2,1)}, u32[]{:S(2)}) copy-start(bf16[2,16,8,2048]{3,2,1,0:T(8,128)(2,1)} %get-tuple-element.230) | copy-start | bytes 3145732
  179.1 3.9 %copy-start = (bf16[128,64,128]{2,0,1:T(8,128)(2,1)S(1)}, bf16[128,64,128]{2,0,1:T(8,128)(2,1)}, u32[]{:S(2)}) copy-start(bf16[128,64,128]{2,0,1:T(8,128)(2,1)} %copy.46) | copy-start | bytes 6291460
  187.8 3.1 %copy-start.14 = (bf16[64,128,128]{2,1,0:T(8,128)(2,1)S(1)}, bf16[64,128,128]{2,1,0:T(8,128)(2,1)}, u32[]{:S(2)}) copy-start(bf16[64,128,128]{2,1,0:T(8,128)(2,1)} %gather_fusion.1) | copy-start | bytes 6291460
  190.9 2.6 %copy-start.13 = (bf16[64,128,128]{2,1,0:T(8,128)(2,1)S(1)}, bf16[64,128,128]{2,1,0:T(8,128)(2,1)}, u32[]{:S(2)}) copy-start(bf16[64,128,128]{2,1,0:T(8,128)(2,1)} %gather_fusion.2) | copy-start | bytes 6291460
  198.3 0.9 copy-start.2
  198.3 0.9 copy-start.12
  198.3 0.9 copy-start.16
  198.3 0.9 copy-start.17
  198.3 0.9 copy-start.18
  214.7 0.6 copy-start.1
  214.7 0.6 copy-start.11
  214.7 0.8 copy-start.15
